TPU v7x, 512 devices: a whole 4x8x8 slice. The times are simulated.
512 devices in a mesh: sec: 2 (over core), atoms: 32 (over z_lo, y), batch: 8 (over z_hi, x).
Axes of the slice: x: 4, y: 8, z: 8 (z_hi: 2, z_lo: 4; z = z_hi * 4 + z_lo), core: 2. Of those that a mesh axis runs over, the one named last changes fastest.
Arguments:
- atoms_in: bfloat16 [8, 16384, 1024], P('batch', 'atoms', 'sec'), may hold values from -6 to 6
- tile_ids: int32 [8, 2, 512], P('batch', None, 'atoms'), may hold values from -1 to 127, as said below
- tile_vals: bfloat16 [8, 512, 128, 128], P('batch', 'atoms'), may hold values from -0.26367188 to 0.26367188
- seq_lens: int32 [8], P('batch'), may hold values from 8193 to 16384, as said below
- pair_labels: int32 [8, 16384], P('batch', 'atoms'), may hold values from 0 to 255
- peak_embed: bfloat16 [8, 256, 256], P('batch', 'sec'), may hold values from -6 to 6
- norm_gain: bfloat16 [1024], P('sec'), may hold values from 0.099609375 to 1.8984375
- w_query: bfloat16 [1024, 512], P(None, 'sec'), may hold values from -0.1875 to 0.1875
- w_key: bfloat16 [1024, 512], P(None, 'sec'), may hold values from -0.1875 to 0.1875
- w_value: bfloat16 [1024, 512], P(None, 'sec'), may hold values from -0.1875 to 0.1875
- w_out: bfloat16 [512, 1024], P('sec'), may hold values from -0.25 to 0.25
- w_proj: bfloat16 [1024, 256], P('sec'), may hold values from -0.1875 to 0.1875
Outputs:
- hidden_two: bfloat16 [8, 16384, 1024], P('batch', 'atoms', 'sec')
- seq_loss: float32 [8], P('batch')
- proj_grad: float32 [8, 1024, 256], P('batch', 'sec')
Inputs may be any that keep to these rules, and one draw needn't show every extreme that they name: `tile_ids`: each index of atoms owns 16 consecutive slots and the row blocks 4 i to 4 (i + 1) - 1; its first 4 slots hold the diagonal tiles of its row blocks; live slots come first and padded slots have both ids -1; every live tile's row block is one of its owner's and its column block lies within 2 blocks of it; in every sequence some index of atoms has all 16 slots live. `seq_lens`: at least one sequence has all 16384 atoms live.
All inputs are finite; a program needn't handle non-finite values.
Results may differ from a plain program's by a relative error of at most 0.013.
Values may be sent and summed in bfloat16 or wider, within the bound.
No kernel may reach another device: no remote copies, remote signals or barrier semaphores. Data moves between devices by JAX's collectives and lax.ppermute only.
A program may use at most 64 MiB of HBM per device.

v0:
```python
import math
import jax
import jax.numpy as jnp
from jax import lax
from jax.sharding import PartitionSpec as P

D = 1024
HEADS = 8
HEAD_DIM = 64
PEAKS = 256
EPSILON = 1e-06
HIGHEST = lax.Precision.HIGHEST


def extended(x, sides, width):
    for axis, dim in sides:
        peers, length = (lax.axis_size(axis), x.shape[dim])
        up = [(i, (i + 1) % peers) for i in range(peers - 1)]
        down = [(j, i) for i, j in up]
        last = lax.slice_in_dim(x, length - width, length, axis=dim)
        leading = lax.slice_in_dim(x, 0, width, axis=dim)
        before = lax.ppermute(last, axis, up)
        after = lax.ppermute(leading, axis, down)
        x = jnp.concatenate([before, x, after], axis=dim)
    return x


def feature_map(values):
    return jax.nn.elu(values) + 1.0


def message_pass(atom_rows, tile_pair, tile_block):
    tile_size = tile_block.shape[-1]
    local_rows, half_width = atom_rows.shape
    block_count = local_rows // tile_size
    reach_blocks = max(block_count // 2, 1)
    padded = extended(atom_rows, (("atoms", 0),), reach_blocks * tile_size)
    blocks = padded.reshape(block_count + 2 * reach_blocks, tile_size, half_width)
    first_block = lax.axis_index("atoms") * block_count
    row_ids = tile_pair[0]
    col_ids = tile_pair[1]
    live_tiles = row_ids >= 0
    col_local = jnp.where(live_tiles, col_ids - first_block + reach_blocks, 0)
    row_local = jnp.where(live_tiles, row_ids - first_block, -1)
    panels = jnp.take(blocks, col_local, axis=0)
    products = jnp.einsum("tij,tjf->tif", tile_block, panels, preferred_element_type=jnp.float32)
    selector = (row_local[None, :] == jnp.arange(block_count, dtype=jnp.int32)[:, None]).astype(
        jnp.float32
    )
    summed = jnp.einsum("bt,tif->bif", selector, products, precision=HIGHEST)
    return summed.reshape(local_rows, half_width).astype(jnp.bfloat16)


def key_summary(key_rows, value_rows, atom_mask, head_count):
    count_rows = key_rows.shape[0]
    feat_keys = (
        feature_map(key_rows.astype(jnp.float32)).reshape(count_rows, head_count, -1)
        * atom_mask[:, None, None]
    )
    value_f = value_rows.astype(jnp.float32).reshape(count_rows, head_count, -1)
    outer_state = jnp.einsum("nhd,nhe->hde", feat_keys, value_f, precision=HIGHEST)
    return (outer_state, jnp.sum(feat_keys, axis=0))


def read_summary(query_rows, outer_state, key_total, head_count):
    count_rows = query_rows.shape[0]
    feat_query = feature_map(query_rows.astype(jnp.float32)).reshape(count_rows, head_count, -1)
    numerator = jnp.einsum("nhd,hde->nhe", feat_query, outer_state, precision=HIGHEST)
    denominator = jnp.einsum("nhd,hd->nh", feat_query, key_total, precision=HIGHEST)
    return (numerator / denominator[..., None]).reshape(count_rows, -1)


def contrast(unit_rows, peak_rows, label_part, mask_part, peak_start):
    logit_scale = 2.0 / math.sqrt(unit_rows.shape[-1])
    peak_f = peak_rows.astype(jnp.float32)
    logits = logit_scale * jnp.dot(unit_rows, peak_f.T, precision=HIGHEST)
    peak_index = peak_start + jnp.arange(peak_rows.shape[0], dtype=jnp.int32)
    target = (label_part[:, None] == peak_index[None, :]).astype(jnp.float32)
    sign_rows = 2.0 * target - 1.0
    loss_part = jnp.sum(mask_part[:, None] * jax.nn.softplus(-sign_rows * logits)) / PEAKS
    slopes = mask_part[:, None] * (jax.nn.sigmoid(logits) - target) * (1.0 / math.sqrt(PEAKS))
    unit_grad = logit_scale * jnp.dot(slopes, peak_f, precision=HIGHEST)
    return (loss_part, unit_grad)


def embed_backward(unit_rows, unit_grad, embed_scale):
    inner_mean = jnp.mean(unit_grad * unit_rows, axis=-1, keepdims=True)
    return (embed_scale * (unit_grad - unit_rows * inner_mean)).astype(jnp.bfloat16)


def shards(
    atoms_in,
    tile_ids,
    tile_vals,
    seq_lens,
    pair_labels,
    peak_embed,
    norm_gain,
    w_query,
    w_key,
    w_value,
    w_out,
    w_proj,
):
    atom_rows = atoms_in[0]
    local_rows = atom_rows.shape[0]
    gathered = message_pass(atom_rows, tile_ids[0], tile_vals[0])
    hidden_one = (atom_rows.astype(jnp.float32) + gathered.astype(jnp.float32)).astype(jnp.bfloat16)
    atom_base = lax.axis_index("atoms") * local_rows
    length_one = seq_lens[0]
    label_row = pair_labels[0]
    peak_part = peak_embed[0]
    hidden_f = hidden_one.astype(jnp.float32)
    square_sum = lax.psum(jnp.sum(hidden_f * hidden_f, axis=-1), "sec")
    row_scale = lax.rsqrt(square_sum[:, None] / D + EPSILON)
    normed = (hidden_f * row_scale * norm_gain.astype(jnp.float32)).astype(jnp.bfloat16)
    head_cols = w_query.shape[1]
    piece_rows = lax.all_gather(normed, "sec", axis=1, tiled=True)
    query_f, key_f, value_f = tuple(
        (
            jnp.dot(piece_rows, weight, preferred_element_type=jnp.float32)
            for weight in (w_query, w_key, w_value)
        )
    )
    head_count = head_cols // HEAD_DIM
    atom_mask = (atom_base + jnp.arange(local_rows, dtype=jnp.int32) < length_one).astype(
        jnp.float32
    )
    outer_state, key_total = key_summary(
        key_f.astype(jnp.bfloat16), value_f.astype(jnp.bfloat16), atom_mask, head_count
    )
    outer_state, key_total = lax.psum((outer_state, key_total), "atoms")
    attended = read_summary(query_f.astype(jnp.bfloat16), outer_state, key_total, head_count)
    out_sum = lax.psum(jnp.sum(attended * attended, axis=-1), "sec")
    attended_n = (attended * lax.rsqrt(out_sum[:, None] / (HEADS * HEAD_DIM) + EPSILON)).astype(
        jnp.bfloat16
    )
    branch_full = jnp.dot(attended_n, w_out, preferred_element_type=jnp.float32)
    branch = lax.psum_scatter(branch_full, "sec", scatter_dimension=1, tiled=True)
    hidden_two = (hidden_f + branch).astype(jnp.bfloat16)
    embedded = lax.psum(jnp.dot(hidden_two, w_proj, preferred_element_type=jnp.float32), "sec")
    embed_scale = lax.rsqrt(jnp.mean(embedded * embedded, axis=-1, keepdims=True) + EPSILON)
    unit_rows = embedded * embed_scale
    peak_start = lax.axis_index("sec") * peak_part.shape[0]
    loss_part, unit_grad = contrast(unit_rows, peak_part, label_row, atom_mask, peak_start)
    unit_grad = lax.psum(unit_grad, "sec")
    embed_grad = embed_backward(unit_rows, unit_grad, embed_scale)
    proj_part = jnp.einsum("nd,ne->de", hidden_two, embed_grad, preferred_element_type=jnp.float32)
    loss_total = lax.psum(loss_part, ("sec", "atoms")) / (local_rows * lax.axis_size("atoms"))
    proj_total = lax.psum(proj_part, "atoms")
    return (hidden_two[None], loss_total.reshape(1), proj_total[None])


def solution(mesh):
    return jax.shard_map(
        shards,
        mesh=mesh,
        in_specs=(
            P("batch", "atoms", "sec"),
            P("batch", None, "atoms"),
            P("batch", "atoms", None, None),
            P("batch"),
            P("batch", "atoms"),
            P("batch", "sec", None),
            P("sec"),
            P(None, "sec"),
            P(None, "sec"),
            P(None, "sec"),
            P("sec", None),
            P("sec", None),
        ),
        out_specs=(P("batch", "atoms", "sec"), P("batch"), P("batch", "sec", None)),
        check_vma=False,
    )
```

profile of v0, /device:TPU:2, one launch (start us, length us, event | category | flops | bytes accessed | tf_op | source)
XLA Modules:
  0.0 773.8 jit_solution(17922998423100423061)
XLA Ops:
  7.2 1.1 slice_bitcast_fusion.1
  8.3 3.5 collective-permute-start
  11.8 1.3 collective-permute-start.1
  13.2 0.8 compare_and_fusion
  13.9 0.7 convert_element_type.72
  14.6 0.7 fusion.57
  15.3 2.1 collective-permute-done
  17.4 4.1 collective-permute-done.1
  21.5 1.1 pad_maximum_fusion
  22.6 2.0 gather_fusion
  24.6 4.4 fusion.2
  29.0 5.5 copy.16
  34.5 3.7 fusion.8
  38.3 0.3 copy.15
  38.6 0.7 copy-done.1
  39.3 0.2 fusion.14
  39.5 2.6 psum.56
  42.1 1.0 fusion.16
  43.2 0.0 all-reduce.5.cloned.1.call-start
  43.9 21.4 %all-gather.2.cloned.1.call-done = bf16[512,1024]{1,0:T(8,128)(2,1)} async-done(((bf16[512,512]{1,0:T(8,128)(2,1)}), bf16[512,1024]{1,0:T(8,128)(2,1)}) %all-gather.2.cloned.1.call-update) | async-done | bytes 1048592 | tf_op jit(solution)/shard_map/all_gather | solution.py:118
  65.3 1.7 convolution_convert_fusion.1
  67.0 2.1 multiply_reduce_fusion.3
  69.1 1.1 fusion.26
  70.2 0.0 reduce-scatter.2.cloned.1.call-start
  70.3 0.1 reduce_sum.58
  70.4 80.4 %psum.58 = f32[4,64]{1,0:T(4,128)S(1)} all-reduce(f32[4,64]{1,0:T(4,128)S(1)} %reduce_sum.58), channel_id=1, replica_groups=mesh['sec'=2,'atoms'=32,'batch'=8] {'atoms'}, use_global_device_ids=true, to_apply=%region_4.5 | all-reduce | flops 256 | bytes 2048 | tf_op jit(solution)/shard_map/psum | solution.py:132
  150.8 1.7 fusion.23
  152.5 0.4 fusion.63
  152.8 197.0 %all-reduce.5.cloned.1.call-done = f32[4,64,64]{1,2,0:T(8,128)} async-done(((f32[4,64,64]{1,2,0:T(8,128)}), f32[4,64,64]{1,2,0:T(8,128)}) %all-reduce.5.cloned.1.call-update) | async-done | bytes 65552 | tf_op jit(solution)/shard_map/psum | solution.py:132
  349.8 1.5 multiply_reduce_fusion.2
  351.3 2.5 psum.59
  353.8 1.8 fusion.64
  355.7 0.0 all-reduce.7.cloned.1.call-start
  355.8 14.7 %reduce-scatter.2.cloned.1.call-done = f32[512,512]{1,0:T(8,128)} async-done(((f32[512,1024]{1,0:T(8,128)}), f32[512,512]{1,0:T(8,128)}) %reduce-scatter.2.cloned.1.call-update) | async-done | bytes 1048592 | tf_op jit(solution)/shard_map/reduce_scatter | solution.py:139
  370.5 1.4 fusion.17
  371.9 1.1 fusion.65
  373.0 0.0 all-reduce.9.cloned.1.call-start
  373.1 37.2 %all-reduce.7.cloned.1.call-done = f32[512,256]{1,0:T(8,128)} async-done(((f32[512,256]{1,0:T(8,128)}), f32[512,256]{1,0:T(8,128)}) %all-reduce.7.cloned.1.call-update) | async-done | bytes 524304 | tf_op jit(solution)/shard_map/psum | solution.py:141
  410.3 1.3 multiply_reduce_fusion.1
  411.6 2.2 fusion.37
  413.8 1.3 convolution_multiply_fusion
  415.1 0.0 all-reduce.11.cloned.1.call-start
  415.1 36.6 %all-reduce.9.cloned.1.call-done = f32[512,256]{1,0:T(8,128)} async-done(((f32[512,256]{1,0:T(8,128)}), f32[512,256]{1,0:T(8,128)}) %all-reduce.9.cloned.1.call-update) | async-done | bytes 524304 | tf_op jit(solution)/shard_map/psum | solution.py:146
  451.7 1.3 multiply_reduce_fusion
  453.0 2.3 convolution_bitcast_fusion
  456.0 141.1 %psum.61 = f32[]{:T(128)} all-reduce(f32[]{:T(128)S(6)} %div.42), channel_id=1, replica_groups=mesh['sec'=2,'atoms'=32,'batch'=8] {'sec','atoms'}, use_global_device_ids=true, to_apply=%region_11.12 | all-reduce | flops 1 | bytes 8 | tf_op jit(solution)/shard_map/psum | solution.py:149
  597.7 166.3 %all-reduce.11.cloned.1.call-done = f32[1,512,256]{2,1,0:T(8,128)} async-done(((f32[1,512,256]{2,1,0:T(8,128)}), f32[1,512,256]{2,1,0:T(8,128)}) %all-reduce.11.cloned.1.call-update) | async-done | bytes 524304 | tf_op jit(solution)/shard_map/psum | solution.py:150
  764.0 1.9 copy.26
  (38 shorter events, 0.3 us)
Async XLA Ops:
  7.2 17.5 %copy-start = (bf16[1,16,128,128]{3,2,1,0:T(8,128)(2,1)S(1)}, bf16[1,16,128,128]{3,2,1,0:T(8,128)(2,1)}, u32[]{:S(2)}) copy-start(bf16[1,16,128,128]{3,2,1,0:T(8,128)(2,1)} %param.14) | copy-start | bytes 1572868
  7.2 58.1 %all-gather.2.cloned.1.call-start = ((), (), s32[]{:S(2)}) async-start(), calls=%async_computation.1 | async-start | bytes 1572864 | tf_op jit(solution)/shard_map/all_gather | solution.py:118
  8.3 9.0 %collective-permute-start = (bf16[256,512]{1,0:T(8,128)(2,1)S(1)}, bf16[256,512]{1,0:T(8,128)(2,1)S(1)}, u32[]{:S(2)}, u32[]{:S(2)}) collective-permute-start(bf16[256,512]{1,0:T(8,128)(2,1)S(1)} %get-tuple-element.7), channel_id=1, source_target_pairs={{0,8},{8,16},{16,24},{24,32},{32,40},{40,48},{48,56},{56,64},{64,7... | collective-permute-start | bytes 786440 | tf_op jit(solution)/shard_map/ppermute | solution.py:22
  11.8 9.7 %collective-permute-start.1 = (bf16[256,512]{1,0:T(8,128)(2,1)S(1)}, bf16[256,512]{1,0:T(8,128)(2,1)S(1)}, u32[]{:S(2)}, u32[]{:S(2)}) collective-permute-start(bf16[256,512]{1,0:T(8,128)(2,1)S(1)} %get-tuple-element.8), channel_id=1, source_target_pairs={{8,0},{16,8},{24,16},{32,24},{40,32},{48,40},{56,48},{64,56},{72,6... | collective-permute-start | bytes 786440 | tf_op jit(solution)/shard_map/ppermute | solution.py:23
  38.3 1.0 copy-start.1
  39.3 26.0 %copy-start.5 = (bf16[1024,256]{1,0:T(8,128)(2,1)S(1)}, bf16[1024,256]{1,0:T(8,128)(2,1)}, u32[]{:S(2)}) copy-start(bf16[1024,256]{1,0:T(8,128)(2,1)} %param.21) | copy-start | bytes 1572868
  39.5 27.5 %copy-start.8 = (bf16[1024,256]{1,0:T(8,128)(2,1)S(1)}, bf16[1024,256]{1,0:T(8,128)(2,1)}, u32[]{:S(2)}) copy-start(bf16[1024,256]{1,0:T(8,128)(2,1)} %param.20) | copy-start | bytes 1572868
  43.2 306.6 %all-reduce.5.cloned.1.call-start = ((), (), s32[]{:S(2)}) async-start(), calls=%async_computation.2 | async-start | bytes 262144 | tf_op jit(solution)/shard_map/psum | solution.py:132
  67.0 83.7 %copy-start.4 = (bf16[512,1024]{1,0:T(8,128)(2,1)S(1)}, bf16[512,1024]{1,0:T(8,128)(2,1)}, u32[]{:S(2)}) copy-start(bf16[512,1024]{1,0:T(8,128)(2,1)} %all-gather.2.cloned.1.call-done) | copy-start | bytes 3145732
  70.2 300.3 %reduce-scatter.2.cloned.1.call-start = ((), (), s32[]{:S(2)}) async-start(), calls=%async_computation.3 | async-start | bytes 3145728 | tf_op jit(solution)/shard_map/reduce_scatter | solution.py:139
  152.4 201.4 %copy-start.6 = (bf16[256,1024]{1,0:T(8,128)(2,1)S(1)}, bf16[256,1024]{1,0:T(8,128)(2,1)}, u32[]{:S(2)}) copy-start(bf16[256,1024]{1,0:T(8,128)(2,1)} %param.22) | copy-start | bytes 1572868
  355.7 16.2 %copy-start.7 = (bf16[512,256]{1,0:T(8,128)(2,1)S(1)}, bf16[512,256]{1,0:T(8,128)(2,1)}, u32[]{:S(2)}) copy-start(bf16[512,256]{1,0:T(8,128)(2,1)} %param.23) | copy-start | bytes 786436
  355.7 55.9 %copy-start.9 = (bf16[1,128,256]{2,1,0:T(8,128)(2,1)S(1)}, bf16[1,128,256]{2,1,0:T(8,128)(2,1)}, u32[]{:S(2)}) copy-start(bf16[1,128,256]{2,1,0:T(8,128)(2,1)} %param.17) | copy-start | bytes 196612
  355.7 55.9 %copy-start.10 = (s32[1,512]{1,0:T(1,128)S(1)}, s32[1,512]{1,0:T(1,128)}, u32[]{:S(2)}) copy-start(s32[1,512]{1,0:T(1,128)} %param.16) | copy-start | bytes 6148
  355.7 54.6 %all-reduce.7.cloned.1.call-start = ((), (), s32[]{:S(2)}) async-start(), calls=%async_computation.4 | async-start | bytes 1048576 | tf_op jit(solution)/shard_map/psum | solution.py:141
  371.9 81.1 %copy-start.3 = (bf16[512,512]{1,0:T(8,128)(2,1)}, bf16[512,512]{1,0:T(8,128)(2,1)S(1)}, u32[]{:S(2)}) copy-start(bf16[512,512]{1,0:T(8,128)(2,1)S(1)} %fusion.17) | copy-start | bytes 1572868
  373.0 78.6 %all-reduce.9.cloned.1.call-start = ((), (), s32[]{:S(2)}) async-start(), calls=%async_computation.5 | async-start | bytes 1048576 | tf_op jit(solution)/shard_map/psum | solution.py:146
  410.3 41.4 %copy-start.2 = (f32[512,256]{1,0:T(8,128)S(1)}, f32[512,256]{1,0:T(8,128)}, u32[]{:S(2)}) copy-start(f32[512,256]{1,0:T(8,128)} %all-reduce.7.cloned.1.call-done) | copy-start | bytes 1572868
  415.1 348.9 %all-reduce.11.cloned.1.call-start = ((), (), s32[]{:S(2)}) async-start(), calls=%async_computation.6 | async-start | bytes 1048576 | tf_op jit(solution)/shard_map/psum | solution.py:150
Sparse Core Ops, SparseCore 0:
  43.3 21.9 all-gather.1
  70.4 279.3 all-reduce.4
  355.8 14.6 reduce-scatter.1
  373.8 36.4 all-reduce.6
  415.2 36.4 all-reduce.8
  455.4 308.4 all-reduce.10
where the time goes:
time: 775 us; the launch traced here: 774 us
  waiting for transfers between devices  479 us (62%)
  blocking collectives  227 us (29%)
  matrix products  25.2 us (3%)
  between operations  17.4 us (2%)
  local copies, waits for them, and re-layouts  11.7 us (2%)
  other arithmetic  8.46 us (1%)
    psum x1, waiting for transfers between devices, shards(): outer_state, key_total = lax.psum((outer_state, key_total), 'atoms')  197 us
    psum x1, waiting for transfers between devices, shards(): proj_total = lax.psum(proj_part, 'atoms')  166 us
    psum x1, blocking collectives, shards(): lax.psum(loss_part, ('sec', 'atoms'))  141 us
    psum x1, blocking collectives, shards(): outer_state, key_total = lax.psum((outer_state, key_total), 'atoms')  80.4 us
    psum x1, waiting for transfers between devices, shards(): lax.psum(jnp.dot(hidden_two, w_proj, preferred_element_type=jnp.float32),...  37.2 us
    psum x1, waiting for transfers between devices, shards(): unit_grad = lax.psum(unit_grad, 'sec')  36.6 us
    all_gather x1, waiting for transfers between devices, shards(): piece_rows = lax.all_gather(normed, 'sec', axis=1, tiled=True)  21.4 us
  transfers between devices with their start and end apart: 8, of which 8 were waited for; matrix products, arithmetic and copies ran while one was open for 1% of the time, Pallas kernels for 0%

commit v1 on v0

--- a/solution.py
+++ b/solution.py
@@ -138,7 +138,10 @@
     branch_full = jnp.dot(attended_n, w_out, preferred_element_type=jnp.float32)
     branch = lax.psum_scatter(branch_full, "sec", scatter_dimension=1, tiled=True)
     hidden_two = (hidden_f + branch).astype(jnp.bfloat16)
-    embedded = lax.psum(jnp.dot(hidden_two, w_proj, preferred_element_type=jnp.float32), "sec")
+    embedded = jnp.sum(
+        lax.all_gather(jnp.dot(hidden_two, w_proj, preferred_element_type=jnp.float32), "sec"),
+        axis=0,
+    )
     embed_scale = lax.rsqrt(jnp.mean(embedded * embedded, axis=-1, keepdims=True) + EPSILON)
     unit_rows = embedded * embed_scale
     peak_start = lax.axis_index("sec") * peak_part.shape[0]

time: 775 us -> 755 us (0.974)
  waiting for transfers between devices: 479 us -> 461 us
    psum x1 -> x0, waiting for transfers between devices: 37.2 us -> none  [shards(): lax.psum(jnp.dot(hidden_two, w_proj, preferred_element_type=jnp.float32),...]
    all_gather x0 -> x1, waiting for transfers between devices: none -> 18.6 us  [shards(): lax.all_gather(jnp.dot(hidden_two, w_proj, preferred_element_type=jnp.flo...]
where the time goes in v1:
time: 755 us; the launch traced here: 754 us
  waiting for transfers between devices  461 us (61%)
  blocking collectives  227 us (30%)
  matrix products  24.2 us (3%)
  between operations  17.4 us (2%)
  local copies, waits for them, and re-layouts  11.7 us (2%)
  other arithmetic  8.7 us (1%)
    psum x1, waiting for transfers between devices, shards(): outer_state, key_total = lax.psum((outer_state, key_total), 'atoms')  197 us
    psum x1, waiting for transfers between devices, shards(): proj_total = lax.psum(proj_part, 'atoms')  166 us
    psum x1, blocking collectives, shards(): lax.psum(loss_part, ('sec', 'atoms'))  141 us
    psum x1, blocking collectives, shards(): outer_state, key_total = lax.psum((outer_state, key_total), 'atoms')  80.4 us
    psum x1, waiting for transfers between devices, shards(): unit_grad = lax.psum(unit_grad, 'sec')  36.6 us
    all_gather x1, waiting for transfers between devices, shards(): piece_rows = lax.all_gather(normed, 'sec', axis=1, tiled=True)  21.4 us
    all_gather x1, waiting for transfers between devices, shards(): lax.all_gather(jnp.dot(hidden_two, w_proj, preferred_element_type=jnp.flo...  18.6 us
  transfers between devices with their start and end apart: 8, of which 8 were waited for; matrix products, arithmetic and copies ran while one was open for 1% of the time, Pallas kernels for 0%

profile of v1, /device:TPU:2, one launch (start us, length us, event | category | flops | bytes accessed | tf_op | source)
XLA Modules:
  0.0 754.4 jit_solution(17879233798281418117)
XLA Ops:
  7.2 1.1 slice_bitcast_fusion.1
  8.3 3.5 collective-permute-start
  11.8 1.3 collective-permute-start.1
  13.2 0.8 compare_and_fusion
  13.9 0.7 convert_element_type.72
  14.6 0.7 fusion.57
  15.3 2.1 collective-permute-done
  17.4 4.1 collective-permute-done.1
  21.5 1.1 pad_maximum_fusion
  22.6 2.0 gather_fusion
  24.6 4.4 fusion.2
  29.0 5.5 copy.16
  34.5 3.7 fusion.8
  38.3 0.3 copy.15
  38.6 0.7 copy-done.1
  39.3 0.2 fusion.14
  39.5 2.6 psum.49
  42.1 1.0 fusion.16
  43.2 0.0 all-reduce.4.cloned.1.call-start
  43.9 21.4 %all-gather.4.cloned.1.call-done = bf16[512,1024]{1,0:T(8,128)(2,1)} async-done(((bf16[512,512]{1,0:T(8,128)(2,1)}), bf16[512,1024]{1,0:T(8,128)(2,1)}) %all-gather.4.cloned.1.call-update) | async-done | bytes 1048592 | tf_op jit(solution)/shard_map/all_gather | solution.py:118
  65.3 1.7 convolution_convert_fusion.1
  67.0 2.1 multiply_reduce_fusion.3
  69.1 1.1 fusion.26
  70.2 0.0 reduce-scatter.2.cloned.1.call-start
  70.3 0.1 reduce_sum.67
  70.4 80.4 %psum.51 = f32[4,64]{1,0:T(4,128)S(1)} all-reduce(f32[4,64]{1,0:T(4,128)S(1)} %reduce_sum.67), channel_id=1, replica_groups=mesh['sec'=2,'atoms'=32,'batch'=8] {'atoms'}, use_global_device_ids=true, to_apply=%region_4.5 | all-reduce | flops 256 | bytes 2048 | tf_op jit(solution)/shard_map/psum | solution.py:132
  150.8 1.7 fusion.23
  152.5 0.4 fusion.63
  152.8 197.0 %all-reduce.4.cloned.1.call-done = f32[4,64,64]{1,2,0:T(8,128)} async-done(((f32[4,64,64]{1,2,0:T(8,128)}), f32[4,64,64]{1,2,0:T(8,128)}) %all-reduce.4.cloned.1.call-update) | async-done | bytes 65552 | tf_op jit(solution)/shard_map/psum | solution.py:132
  349.8 1.5 multiply_reduce_fusion.2
  351.3 2.5 psum.52
  353.8 1.8 fusion.64
  355.8 14.8 %reduce-scatter.2.cloned.1.call-done = f32[512,512]{1,0:T(8,128)} async-done(((f32[512,1024]{1,0:T(8,128)}), f32[512,512]{1,0:T(8,128)}) %reduce-scatter.2.cloned.1.call-update) | async-done | bytes 1048592 | tf_op jit(solution)/shard_map/reduce_scatter | solution.py:139
  370.5 1.4 fusion.17
  371.9 1.1 fusion.65
  373.1 0.0 all-reduce.6.cloned.1.call-start
  373.1 18.6 %all-gather.6.cloned.1.call-done = f32[1024,256]{1,0:T(8,128)} async-done(((f32[512,256]{1,0:T(8,128)}), f32[1024,256]{1,0:T(8,128)}) %all-gather.6.cloned.1.call-update) | async-done | bytes 1048592 | tf_op jit(solution)/shard_map/all_gather | solution.py:142
  391.7 1.4 reduce_sum.69
  393.1 0.1 multiply_reduce_fusion.1
  393.2 1.1 fusion.37
  394.4 1.3 convolution_multiply_fusion
  395.6 0.0 all-reduce.8.cloned.1.call-start
  395.7 36.6 %all-reduce.6.cloned.1.call-done = f32[512,256]{1,0:T(8,128)} async-done(((f32[512,256]{1,0:T(8,128)}), f32[512,256]{1,0:T(8,128)}) %all-reduce.6.cloned.1.call-update) | async-done | bytes 524304 | tf_op jit(solution)/shard_map/psum | solution.py:149
  432.2 1.3 multiply_reduce_fusion
  433.5 2.3 convolution_bitcast_fusion
  436.5 141.1 %psum.53 = f32[]{:T(128)} all-reduce(f32[]{:T(128)S(6)} %div.42), channel_id=1, replica_groups=mesh['sec'=2,'atoms'=32,'batch'=8] {'sec','atoms'}, use_global_device_ids=true, to_apply=%region_11.12 | all-reduce | flops 1 | bytes 8 | tf_op jit(solution)/shard_map/psum | solution.py:152
  578.3 166.3 %all-reduce.8.cloned.1.call-done = f32[1,512,256]{2,1,0:T(8,128)} async-done(((f32[1,512,256]{2,1,0:T(8,128)}), f32[1,512,256]{2,1,0:T(8,128)}) %all-reduce.8.cloned.1.call-update) | async-done | bytes 524304 | tf_op jit(solution)/shard_map/psum | solution.py:153
  744.5 1.9 copy.25
  (37 shorter events, 0.3 us)
Async XLA Ops:
  7.2 17.5 %copy-start = (bf16[1,16,128,128]{3,2,1,0:T(8,128)(2,1)S(1)}, bf16[1,16,128,128]{3,2,1,0:T(8,128)(2,1)}, u32[]{:S(2)}) copy-start(bf16[1,16,128,128]{3,2,1,0:T(8,128)(2,1)} %param.14) | copy-start | bytes 1572868
  7.2 58.1 %all-gather.4.cloned.1.call-start = ((), (), s32[]{:S(2)}) async-start(), calls=%async_computation.1 | async-start | bytes 1572864 | tf_op jit(solution)/shard_map/all_gather | solution.py:118
  8.3 9.0 %collective-permute-start = (bf16[256,512]{1,0:T(8,128)(2,1)S(1)}, bf16[256,512]{1,0:T(8,128)(2,1)S(1)}, u32[]{:S(2)}, u32[]{:S(2)}) collective-permute-start(bf16[256,512]{1,0:T(8,128)(2,1)S(1)} %get-tuple-element.7), channel_id=1, source_target_pairs={{0,8},{8,16},{16,24},{24,32},{32,40},{40,48},{48,56},{56,64},{64,7... | collective-permute-start | bytes 786440 | tf_op jit(solution)/shard_map/ppermute | solution.py:22
  11.8 9.7 %collective-permute-start.1 = (bf16[256,512]{1,0:T(8,128)(2,1)S(1)}, bf16[256,512]{1,0:T(8,128)(2,1)S(1)}, u32[]{:S(2)}, u32[]{:S(2)}) collective-permute-start(bf16[256,512]{1,0:T(8,128)(2,1)S(1)} %get-tuple-element.8), channel_id=1, source_target_pairs={{8,0},{16,8},{24,16},{32,24},{40,32},{48,40},{56,48},{64,56},{72,6... | collective-permute-start | bytes 786440 | tf_op jit(solution)/shard_map/ppermute | solution.py:23
  38.3 1.0 copy-start.1
  39.3 26.0 %copy-start.4 = (bf16[1024,256]{1,0:T(8,128)(2,1)S(1)}, bf16[1024,256]{1,0:T(8,128)(2,1)}, u32[]{:S(2)}) copy-start(bf16[1024,256]{1,0:T(8,128)(2,1)} %param.21) | copy-start | bytes 1572868
  39.5 27.5 %copy-start.7 = (bf16[1024,256]{1,0:T(8,128)(2,1)S(1)}, bf16[1024,256]{1,0:T(8,128)(2,1)}, u32[]{:S(2)}) copy-start(bf16[1024,256]{1,0:T(8,128)(2,1)} %param.20) | copy-start | bytes 1572868
  43.2 306.6 %all-reduce.4.cloned.1.call-start = ((), (), s32[]{:S(2)}) async-start(), calls=%async_computation.2 | async-start | bytes 262144 | tf_op jit(solution)/shard_map/psum | solution.py:132
  67.0 83.7 %copy-start.3 = (bf16[512,1024]{1,0:T(8,128)(2,1)S(1)}, bf16[512,1024]{1,0:T(8,128)(2,1)}, u32[]{:S(2)}) copy-start(bf16[512,1024]{1,0:T(8,128)(2,1)} %all-gather.4.cloned.1.call-done) | copy-start | bytes 3145732
  70.2 300.3 %reduce-scatter.2.cloned.1.call-start = ((), (), s32[]{:S(2)}) async-start(), calls=%async_computation.3 | async-start | bytes 3145728 | tf_op jit(solution)/shard_map/reduce_scatter | solution.py:139
  152.4 201.4 %copy-start.5 = (bf16[256,1024]{1,0:T(8,128)(2,1)S(1)}, bf16[256,1024]{1,0:T(8,128)(2,1)}, u32[]{:S(2)}) copy-start(bf16[256,1024]{1,0:T(8,128)(2,1)} %param.22) | copy-start | bytes 1572868
  355.7 16.2 %copy-start.6 = (bf16[512,256]{1,0:T(8,128)(2,1)S(1)}, bf16[512,256]{1,0:T(8,128)(2,1)}, u32[]{:S(2)}) copy-start(bf16[512,256]{1,0:T(8,128)(2,1)} %param.23) | copy-start | bytes 786436
  355.7 36.0 %all-gather.6.cloned.1.call-start = ((), (), s32[]{:S(2)}) async-start(), calls=%async_computation.6 | async-start | bytes 1572864 | tf_op jit(solution)/shard_map/all_gather | solution.py:142
  371.9 61.6 %copy-start.2 = (bf16[512,512]{1,0:T(8,128)(2,1)}, bf16[512,512]{1,0:T(8,128)(2,1)S(1)}, u32[]{:S(2)}) copy-start(bf16[512,512]{1,0:T(8,128)(2,1)S(1)} %fusion.17) | copy-start | bytes 1572868
  371.9 21.3 %copy-start.8 = (bf16[1,128,256]{2,1,0:T(8,128)(2,1)S(1)}, bf16[1,128,256]{2,1,0:T(8,128)(2,1)}, u32[]{:S(2)}) copy-start(bf16[1,128,256]{2,1,0:T(8,128)(2,1)} %param.17) | copy-start | bytes 196612
  371.9 21.3 %copy-start.9 = (s32[1,512]{1,0:T(1,128)S(1)}, s32[1,512]{1,0:T(1,128)}, u32[]{:S(2)}) copy-start(s32[1,512]{1,0:T(1,128)} %param.16) | copy-start | bytes 6148
  373.1 59.2 %all-reduce.6.cloned.1.call-start = ((), (), s32[]{:S(2)}) async-start(), calls=%async_computation.4 | async-start | bytes 1048576 | tf_op jit(solution)/shard_map/psum | solution.py:149
  395.6 348.9 %all-reduce.8.cloned.1.call-start = ((), (), s32[]{:S(2)}) async-start(), calls=%async_computation.5 | async-start | bytes 1048576 | tf_op jit(solution)/shard_map/psum | solution.py:153
Sparse Core Ops, SparseCore 0:
  43.3 21.9 all-gather.3
  70.4 279.3 all-reduce.3
  355.8 14.6 reduce-scatter.1
  373.2 18.4 all-gather.5
  395.8 36.4 all-reduce.5
  436.0 308.4 all-reduce.7
